TPU v7x, 512 devices: a whole 4x8x8 slice. The times are simulated.
512 devices in a mesh: depth: 16 (over z_lo, x, core), height: 8 (over y), sample: 4 (over z_hi).
Axes of the slice: x: 4, y: 8, z: 8 (z_hi: 4, z_lo: 2; z = z_hi * 2 + z_lo), core: 2. Of those that a mesh axis runs over, the one named last changes fastest.
Arguments:
- volume: bfloat16 [4, 4, 64, 32, 512], P('sample', None, 'depth', 'height'), may hold values from -6 to 6
- kernel_one: bfloat16 [32, 108], replicated, may hold values from -0.625 to 0.625
- kernel_two: bfloat16 [64, 864], P('height'), may hold values from -0.21875 to 0.21875
- cotangent: bfloat16 [4, 64, 16, 1024], P('sample', 'height', 'depth'), may hold values from -24 to 24
Outputs:
- pooled_two: bfloat16 [4, 64, 16, 1024], P('sample', 'height', 'depth')
- weight_grad: float32 [64, 864], P('height')
- act_grad: bfloat16 [4, 32, 32, 16, 256], P('sample', None, 'depth', 'height')
All inputs are finite; a program needn't handle non-finite values.
Results may differ from a plain program's by a relative error of at most 0.005.
Values may be sent and summed in bfloat16 or wider, within the bound.
No kernel may reach another device: no remote copies, remote signals or barrier semaphores. Data moves between devices by JAX's collectives and lax.ppermute only.
A program may use at most 64 MiB of HBM per device.

v0:
```python
import jax
import jax.numpy as jnp
from jax import lax
from jax.sharding import PartitionSpec as P

LEAK_SLOPE = 0.3
CONV_DIMS = ("NCDHW", "OIDHW", "NCDHW")


def extended(block, sides, width):
    for axis, dim in sides:
        count = lax.axis_size(axis)
        forward = [(i, i + 1) for i in range(count - 1)]
        backward = [(target, source) for source, target in forward]
        low = lax.ppermute(
            lax.slice_in_dim(block, block.shape[dim] - width, None, axis=dim), axis, forward
        )
        high = lax.ppermute(lax.slice_in_dim(block, 0, width, axis=dim), axis, backward)
        block = jnp.concatenate([low, block, high], axis=dim)
    return block


def butterfly_sum(values, axes):
    sizes = [lax.axis_size(axis) for axis in axes]
    count = 1
    for size in sizes:
        count *= size
    if count & count - 1:
        return lax.psum(values, axes)
    inner = lax.axis_size(axes[-1])

    def label(i):
        low = i % inner
        i = i - low + (low ^ low >> 1)
        mid = i // (inner * 2) % 4
        return i + ((mid ^ mid >> 1) - mid) * inner * 2

    owner = {label(i): i for i in range(count)}
    step = 1
    while step < count:
        pairs = [(i, owner[label(i) ^ step]) for i in range(count)]
        values = values + lax.ppermute(values, axes, pairs)
        step *= 2
    return values


def halving_scatter(values, axis, dim):
    count = lax.axis_size(axis)
    if count & count - 1:
        return lax.psum_scatter(values, axis, scatter_dimension=dim, tiled=True)
    index = lax.axis_index(axis)
    step = count // 2
    while step >= 1:
        half = values.shape[dim] // 2
        bit = index // step % 2
        keep = lax.dynamic_slice_in_dim(values, bit * half, half, axis=dim)
        send = lax.dynamic_slice_in_dim(values, (1 - bit) * half, half, axis=dim)
        pairs = [(i, i ^ step) for i in range(count)]
        values = keep + lax.ppermute(send, axis, pairs)
        step //= 2
    return values


def delta_shifts(delta_ext):
    _, _, _, hsize, wsize = delta_ext.shape
    dpad = jnp.pad(delta_ext[0], ((0, 0), (0, 0), (1, 1), (1, 1)))
    return jnp.stack(
        [
            dpad[:, :, 2 - kh : 2 - kh + hsize, 2 - kw : 2 - kw + wsize]
            for kh in range(3)
            for kw in range(3)
        ],
        axis=1,
    )


def weight_gradient(level_ext, shifted):
    chans = level_ext.shape[1]
    filters, _, dsize, _, _ = shifted.shape
    levels = jnp.stack([level_ext[0, :, kd : kd + dsize] for kd in range(3)], axis=0)
    grad = lax.dot_general(
        shifted, levels, (((2, 3, 4), (2, 3, 4)), ((), ())), preferred_element_type=jnp.float32
    )
    grad = grad.reshape(filters, 3, 3, 3, chans)
    return jnp.transpose(grad, (0, 4, 3, 1, 2)).reshape(filters, chans * 27)


def back_product(shifts_ext, kernel):
    filters, chans = kernel.shape[:2]
    dsize = shifts_ext.shape[2] - 2
    stacked = jnp.stack([shifts_ext[:, :, 2 - kd : 2 - kd + dsize] for kd in range(3)], axis=0)
    weights = jnp.transpose(kernel, (1, 2, 0, 3, 4)).reshape(chans, 3, filters, 9)
    grad = lax.dot_general(
        weights, stacked, (((1, 2, 3), (0, 1, 2)), ((), ())), preferred_element_type=jnp.float32
    )
    return grad[None]


def forward_product(level_ext, kernel):
    filters, chans = kernel.shape[:2]
    dsize = level_ext.shape[2] - 2
    shifts = delta_shifts(level_ext)
    stacked = jnp.stack([shifts[:, :, kd : kd + dsize] for kd in range(3)], axis=0)
    flipped = jnp.flip(kernel, axis=(3, 4))
    weights = jnp.transpose(flipped, (0, 2, 1, 3, 4)).reshape(filters, 3, chans, 9)
    grad = lax.dot_general(
        weights, stacked, (((1, 2, 3), (0, 1, 2)), ((), ())), preferred_element_type=jnp.float32
    )
    return grad[None]


def near_first_scatter(values, axis):
    count = lax.axis_size(axis)
    chans, dsize, hsize, wsize = values.shape[1:]
    if count & count - 1:
        return lax.psum_scatter(values, axis, scatter_dimension=3, tiled=True)
    bits = count.bit_length() - 1
    rows = hsize // count
    index = lax.axis_index(axis)
    grid = jnp.transpose(values[0], (2, 1, 0, 3))
    grid = grid.reshape((2,) * bits + (rows, dsize, chans, wsize))
    for t in range(bits):
        axis_pos = bits - 1 - t
        bit = index >> t & 1
        keep = lax.dynamic_slice_in_dim(grid, bit, 1, axis=axis_pos)
        send = lax.dynamic_slice_in_dim(grid, 1 - bit, 1, axis=axis_pos)
        pairs = [(i, i ^ 1 << t) for i in range(count)]
        grid = jnp.squeeze(keep + lax.ppermute(send, axis, pairs), axis_pos)
    return jnp.transpose(grid, (2, 1, 0, 3))[None]


def activate(values):
    return LEAK_SLOPE * values + (1.0 - LEAK_SLOPE) * jax.nn.softplus(values)


def slope_at(values):
    return LEAK_SLOPE + (1.0 - LEAK_SLOPE) * jax.nn.sigmoid(values)


def pooled(values):
    count, chans, dsize, hsize, wsize = values.shape
    blocks = values.reshape(count, chans, dsize // 2, 2, hsize // 2, 2, wsize // 2, 2)
    return blocks.mean(axis=(3, 5, 7))


def spread_up(values):
    values = jnp.repeat(jnp.repeat(jnp.repeat(values, 2, axis=2), 2, axis=3), 2, axis=4)
    return values * 0.125


def conv_valid(inputs, kernel):
    return lax.conv_general_dilated(
        inputs,
        kernel,
        (1, 1, 1),
        "VALID",
        dimension_numbers=CONV_DIMS,
        preferred_element_type=jnp.float32,
    )


def back_conv(delta_pad, kernel):
    flipped = jnp.flip(kernel, axis=(2, 3, 4))
    return lax.conv_general_dilated(
        delta_pad,
        flipped,
        (1, 1, 1),
        "VALID",
        dimension_numbers=("NCDHW", "IODHW", "NCDHW"),
        preferred_element_type=jnp.float32,
    )


def shards(volume, kernel_one, kernel_two, cotangent):
    depth_count = lax.axis_size("depth")
    height_count = lax.axis_size("height")
    sample_count = lax.axis_size("sample")
    chans_in = volume.shape[1]
    depth_loc = volume.shape[2]
    height_loc = volume.shape[3]
    width_all = volume.shape[4]
    chans_mid = kernel_one.shape[0]
    filters = kernel_two.shape[0]
    first_kernel = kernel_one.reshape(chans_mid, chans_in, 3, 3, 3)
    second_kernel = kernel_two.reshape(filters, chans_mid, 3, 3, 3)
    padded = extended(volume, (("depth", 2), ("height", 3)), 1)
    pre_one = forward_product(padded, first_kernel)[:, :, :, 1:-1]
    level_loc = pooled(activate(pre_one)).astype(jnp.bfloat16)
    slab_rows = lax.all_gather(level_loc, "height", axis=3, tiled=True)
    level_one = extended(slab_rows, (("depth", 2),), 1)
    pre_two = forward_product(level_one, second_kernel)
    pooled_grid = pooled(activate(pre_two)).astype(jnp.bfloat16)
    depth_two = pooled_grid.shape[2]
    pooled_two = pooled_grid.reshape(
        1, filters, depth_two, pooled_grid.shape[3] * pooled_grid.shape[4]
    )
    cot_grid = cotangent.reshape(1, filters, depth_two, pooled_grid.shape[3], pooled_grid.shape[4])
    delta_two = (spread_up(cot_grid.astype(jnp.float32)) * slope_at(pre_two)).astype(jnp.bfloat16)
    scale = (
        1.0
        / float(
            sample_count
            * (depth_loc // 2)
            * depth_count
            * (height_loc // 2)
            * height_count
            * (width_all // 2)
        )
        ** 0.5
    )
    delta_ext = extended(delta_two, (("depth", 2),), 1)
    shifts_ext = delta_shifts(delta_ext)
    weight_term = weight_gradient(level_one, delta_shifts(delta_two)) * scale
    flat_size = weight_term.size
    lanes = 128 if flat_size % 128 == 0 else flat_size
    weight_grad = butterfly_sum(
        weight_term.reshape(flat_size // lanes, lanes), ("depth", "sample")
    ).reshape(weight_term.shape)
    back_part = back_product(shifts_ext, second_kernel)
    act_grad = near_first_scatter(back_part, "height").astype(jnp.bfloat16)
    return (pooled_two, weight_grad, act_grad)


def solution(mesh):
    in_specs = (
        P("sample", None, "depth", "height", None),
        P(),
        P("height", None),
        P("sample", "height", "depth", None),
    )
    out_specs = (
        P("sample", "height", "depth", None),
        P("height", None),
        P("sample", None, "depth", "height", None),
    )
    return jax.shard_map(shards, mesh=mesh, in_specs=in_specs, out_specs=out_specs, check_vma=False)
```

profile of v0, /device:TPU:8, one launch (start us, length us, event | category | flops | bytes accessed | tf_op | source)
XLA Modules:
  0.0 182.4 jit_solution(10404301565494377352)
XLA Ops:
  0.6 0.8 fusion.119
  1.4 1.7 collective-permute-start
  3.1 1.3 collective-permute-start.1
  4.5 0.9 constant_dynamic-update-slice_fusion.1
  5.3 2.2 %collective-permute-done.1 = bf16[1,4,1,4,512]{4,3,2,1,0:T(4,128)(2,1)S(1)} collective-permute-done((bf16[1,4,1,4,512]{4,3,2,1,0:T(4,128)(2,1)S(1)}, bf16[1,4,1,4,512]{4,3,2,1,0:T(4,128)(2,1)S(1)}, u32[]{:S(2)}, u32[]{:S(2)}) %collective-permute-start.1) | collective-permute-done | bytes 16416 | tf_op jit(solution)/shard_map/ppermute | solution.py:18
  7.6 3.5 %collective-permute-start.2 = (bf16[1,4,6,1,512]{4,3,2,1,0:T(2,128)(2,1)S(1)}, bf16[1,4,6,1,512]{4,3,2,1,0:T(2,128)(2,1)S(1)}, u32[]{:S(2)}, u32[]{:S(2)}) collective-permute-start(bf16[1,4,6,1,512]{4,3,2,1,0:T(2,128)(2,1)S(1)} %get-tuple-element.57), channel_id=1, source_target_pairs={{0,4},{4,8},{8,12},{12,16},{16,20},{20,24},{24,28},{1,5},{5,9},{9,... | collective-permute-start | bytes 73736 | tf_op jit(solution)/shard_map/ppermute | solution.py:15
  11.1 3.8 %collective-permute-start.3 = (bf16[1,4,6,1,512]{4,3,2,1,0:T(2,128)(2,1)S(1)}, bf16[1,4,6,1,512]{4,3,2,1,0:T(2,128)(2,1)S(1)}, u32[]{:S(2)}, u32[]{:S(2)}) collective-permute-start(bf16[1,4,6,1,512]{4,3,2,1,0:T(2,128)(2,1)S(1)} %get-tuple-element.58), channel_id=1, source_target_pairs={{4,0},{8,4},{12,8},{16,12},{20,16},{24,20},{28,24},{5,1},{9,5},{13... | collective-permute-start | bytes 73736 | tf_op jit(solution)/shard_map/ppermute | solution.py:18
  14.9 0.8 copy.389
  15.8 0.6 copy.390
  16.4 0.6 collective-permute-done.3
  17.2 0.7 fusion.89
  18.9 0.9 copy.383
  19.9 0.9 copy.384
  20.8 1.0 copy.385
  21.8 0.9 copy.386
  22.7 0.9 copy.382
  23.7 11.4 %stack.168 = bf16[4,9,6,6,512]{4,1,0,3,2:T(8,128)(2,1)S(1)} concatenate(bf16[4,1,6,6,512]{4,1,0,3,2:T(2,128)(2,1)S(1)} %copy.378, bf16[4,1,6,6,512]{4,1,0,3,2:T(2,128)(2,1)S(1)} %copy.379, bf16[4,1,6,6,512]{4,1,0,3,2:T(2,128)(2,1)S(1)} %copy.380, bf16[4,1,6,6,512]{4,1,0,3,2:T(2,128)(2,1)S(1)} %copy.381, bf16[4,1,6,6,512]{4,1,0,3,2:T(2,128)(2,1)} %copy.382, ...), dimensions={1} | concatenate | bytes 2654208 | tf_op jit(solution)/shard_map/stack | solution.py:67
  35.1 0.6 slice_bitcast_fusion.5
  35.9 1.4 fusion.27
  37.2 0.6 fusion.61
  37.9 2.6 %copy.392 = f32[1,32,4,4,512]{1,4,3,2,0:T(8,128)} copy(f32[1,32,4,4,512]{4,1,3,2,0:T(8,128)S(1)} %fusion.61) | data formatting | bytes 2097152 | tf_op jit(solution)/shard_map/add | solution.py:133
  40.5 4.8 %reduce_sum.21 = f32[32,2,2,256]{0,3,2,1:T(8,128)S(1)} reduce(f32[32,2,2,2,2,256,2]{0,6,5,4,3,2,1:T(2,128)} %bitcast.266, f32[]{:T(128)} %constant.17.clone.1), dimensions={2,4,6}, to_apply=%region_0.1 | reduce | flops 229376 | bytes 1179652 | tf_op jit(solution)/shard_map/reduce_sum | solution.py:143
  45.5 27.9 %all-gather = bf16[32,2,16,256]{3,0,2,1:T(8,128)(2,1)S(1)} all-gather(bf16[32,2,2,256]{3,0,2,1:T(8,128)(2,1)S(1)} %multiply_convert_fusion.2), channel_id=2, replica_groups=mesh['depth'=16,'height'=8,'sample'=4] {'height'}, dimensions={2}, use_global_device_ids=true | all-gather | bytes 589824 | tf_op jit(solution)/shard_map/all_gather | solution.py:189
  73.5 1.3 collective-permute-start.4
  74.8 1.5 collective-permute-start.5
  76.6 0.7 rev.9
  77.3 0.8 copy.405
  79.1 1.7 collective-permute-done.5
  81.4 0.4 fusion.49
  81.8 0.4 fusion.51
  82.3 0.5 fusion.53
  83.3 0.4 fusion.59
  83.8 2.8 %slice_bitcast_fusion.2 = (bf16[1,32,9,2,16,256]{5,1,2,0,4,3:T(8,128)(2,1)S(1)}, bf16[1,32,9,2,16,256]{5,1,2,0,4,3:T(8,128)(2,1)S(1)}, bf16[1,32,9,2,16,256]{5,1,2,0,4,3:T(8,128)(2,1)S(1)}) fusion(bf16[32,9,4,16,256]{4,0,1,3,2:T(8,128)(2,1)S(1)} %fusion.59), kind=kLoop, calls=%fused_computation.8 | loop fusion | bytes 28311552 | tf_op jit(solution)/shard_map/stack | solution.py:103
  86.5 2.6 %multiply_convert_fusion.1 = (bf16[8,2,16,256]{3,0,2,1:T(8,128)(2,1)S(1)}, f32[8,16,256]{2,0,1:T(8,128)S(1)}) fusion(f32[8,16,256]{2,0,1:T(8,128)S(1)} %copy.408, bf16[8,3,32,9,1,1]{2,0,3,1,5,4:T(8,128)(2,1)S(1)} %bitcast.281, bf16[1,32,9,2,16,256]{5,1,2,0,4,3:T(8,128)(2,1)S(1)} %get-tuple-element.31, ...), kind=kOutput, calls=%fused_computation.113 | convolution fusion | flops 128483328 | bytes 14562816 | tf_op jit(solution)/shard_map/dot_general | solution.py:106
  89.3 6.7 %collective-permute-start.12 = (bf16[1,8,1,16,256]{4,1,3,2,0:T(8,128)(2,1)S(1)}, bf16[1,8,1,16,256]{4,1,3,2,0:T(8,128)(2,1)S(1)}, u32[]{:S(2)}, u32[]{:S(2)}) collective-permute-start(bf16[1,8,1,16,256]{4,1,3,2,0:T(8,128)(2,1)S(1)} %get-tuple-element.55), channel_id=1, source_target_pairs={{0,32},{32,64},{64,96},{96,128},{128,160},{160,192},{192,224},{224... | collective-permute-start | bytes 196616 | tf_op jit(solution)/shard_map/ppermute | solution.py:15
  96.0 1.3 collective-permute-start.13
  97.6 1.6 collective-permute-done.13
  100.5 0.9 fusion.12
  101.6 1.9 %collective-permute-start.14 = (f32[2,2,1,2,2,32,256]{6,5,4,3,0,2,1:T(8,128)S(1)}, f32[2,2,1,2,2,32,256]{6,5,4,3,0,2,1:T(8,128)S(1)}, u32[]{:S(2)}, u32[]{:S(2)}) collective-permute-start(f32[2,2,1,2,2,32,256]{6,5,4,3,0,2,1:T(8,128)S(1)} %copy.444), channel_id=1, source_target_pairs={{0,4},{4,0},{8,12},{12,8},{16,20},{20,16},{24,28},{28,24},{1,5},{5... | collective-permute-start | bytes 1572872 | tf_op jit(solution)/shard_map/ppermute | solution.py:128
  103.9 12.7 %collective-permute-done.14 = f32[2,2,1,2,2,32,256]{6,5,4,3,0,2,1:T(8,128)S(1)} collective-permute-done((f32[2,2,1,2,2,32,256]{6,5,4,3,0,2,1:T(8,128)S(1)}, f32[2,2,1,2,2,32,256]{6,5,4,3,0,2,1:T(8,128)S(1)}, u32[]{:S(2)}, u32[]{:S(2)}) %collective-permute-start.14) | collective-permute-done | bytes 524320 | tf_op jit(solution)/shard_map/ppermute | solution.py:128
  116.7 4.6 %collective-permute-start.15 = (f32[2,1,2,2,32,256]{5,4,3,2,0,1:T(8,128)S(1)}, f32[2,1,2,2,32,256]{5,4,3,2,0,1:T(8,128)}, u32[]{:S(2)}, u32[]{:S(2)}) collective-permute-start(f32[2,1,2,2,32,256]{5,4,3,2,0,1:T(8,128)S(1)} %dynamic-slice_bitcast_fusion), channel_id=1, source_target_pairs={{0,8},{4,12},{8,0},{12,4},{16,24},{20,28},{24,16},{28,20},{1,9},{5... | collective-permute-start | bytes 786440 | tf_op jit(solution)/shard_map/ppermute | solution.py:128
  121.2 1.2 fusion.39
  122.5 1.2 copy.409
  123.7 1.0 mul.80
  124.7 6.1 %collective-permute-start.6 = (f32[54,128]{1,0:T(8,128)S(1)}, f32[54,128]{1,0:T(8,128)S(1)}, u32[]{:S(2)}, u32[]{:S(2)}) collective-permute-start(f32[54,128]{1,0:T(8,128)S(1)} %mul.80), channel_id=1, source_target_pairs={{0,1},{1,0},{2,3},{3,2},{32,33},{33,32},{34,35},{35,34},{64,65},{6... | collective-permute-start | bytes 82952 | tf_op jit(solution)/shard_map/ppermute | solution.py:42
  130.8 1.8 %collective-permute-done.6 = f32[54,128]{1,0:T(8,128)S(1)} collective-permute-done((f32[54,128]{1,0:T(8,128)S(1)}, f32[54,128]{1,0:T(8,128)S(1)}, u32[]{:S(2)}, u32[]{:S(2)}) %collective-permute-start.6) | collective-permute-done | bytes 27680 | tf_op jit(solution)/shard_map/ppermute | solution.py:42
  132.6 9.7 %collective-permute-start.7 = (f32[54,128]{1,0:T(8,128)S(1)}, f32[54,128]{1,0:T(8,128)S(1)}, u32[]{:S(2)}, u32[]{:S(2)}) collective-permute-start(f32[54,128]{1,0:T(8,128)S(1)} %add.86), channel_id=1, source_target_pairs={{0,3},{1,2},{2,1},{3,0},{32,35},{33,34},{34,33},{35,32},{64,67},{6... | collective-permute-start | bytes 82952 | tf_op jit(solution)/shard_map/ppermute | solution.py:42
  142.3 1.8 %collective-permute-done.7 = f32[54,128]{1,0:T(8,128)S(1)} collective-permute-done((f32[54,128]{1,0:T(8,128)S(1)}, f32[54,128]{1,0:T(8,128)S(1)}, u32[]{:S(2)}, u32[]{:S(2)}) %collective-permute-start.7) | collective-permute-done | bytes 27680 | tf_op jit(solution)/shard_map/ppermute | solution.py:42
  144.1 1.9 %collective-permute-start.8 = (f32[54,128]{1,0:T(8,128)S(1)}, f32[54,128]{1,0:T(8,128)S(1)}, u32[]{:S(2)}, u32[]{:S(2)}) collective-permute-start(f32[54,128]{1,0:T(8,128)S(1)} %add.87), channel_id=1, source_target_pairs={{0,32},{1,33},{2,34},{3,35},{32,0},{33,1},{34,2},{35,3},{64,96},{6... | collective-permute-start | bytes 82952 | tf_op jit(solution)/shard_map/ppermute | solution.py:42
  146.0 1.2 collective-permute-done.8
  147.2 5.3 %collective-permute-start.9 = (f32[54,128]{1,0:T(8,128)S(1)}, f32[54,128]{1,0:T(8,128)S(1)}, u32[]{:S(2)}, u32[]{:S(2)}) collective-permute-start(f32[54,128]{1,0:T(8,128)S(1)} %add.88), channel_id=1, source_target_pairs={{0,64},{1,65},{2,66},{3,67},{32,96},{33,97},{34,98},{35,99},{64,0}... | collective-permute-start | bytes 82952 | tf_op jit(solution)/shard_map/ppermute | solution.py:42
  152.6 1.8 %collective-permute-done.9 = f32[54,128]{1,0:T(8,128)S(1)} collective-permute-done((f32[54,128]{1,0:T(8,128)S(1)}, f32[54,128]{1,0:T(8,128)S(1)}, u32[]{:S(2)}, u32[]{:S(2)}) %collective-permute-start.9) | collective-permute-done | bytes 27680 | tf_op jit(solution)/shard_map/ppermute | solution.py:42
  154.4 0.6 add.89
  155.0 7.0 %collective-permute-start.10 = (f32[54,128]{1,0:T(8,128)}, f32[54,128]{1,0:T(8,128)}, u32[]{:S(2)}, u32[]{:S(2)}) collective-permute-start(f32[54,128]{1,0:T(8,128)} %add.89), channel_id=1, source_target_pairs={{0,192},{1,193},{2,194},{3,195},{32,224},{33,225},{34,226},{35,227... | collective-permute-start | bytes 82952 | tf_op jit(solution)/shard_map/ppermute | solution.py:42
  162.0 0.6 copy.406
  162.6 1.7 reduce_sum.28
  164.3 0.8 add.90
  165.1 3.4 %collective-permute-start.11 = (f32[54,128]{1,0:T(8,128)S(1)}, f32[54,128]{1,0:T(8,128)S(1)}, u32[]{:S(2)}, u32[]{:S(2)}) collective-permute-start(f32[54,128]{1,0:T(8,128)S(1)} %add.90), channel_id=1, source_target_pairs={{0,256},{1,257},{2,258},{3,259},{32,288},{33,289},{34,290},{35,291... | collective-permute-start | bytes 82952 | tf_op jit(solution)/shard_map/ppermute | solution.py:42
  168.5 1.0 bitcast_add_fusion
  169.5 4.6 %collective-permute-start.16 = (f32[1,2,2,32,256]{4,3,2,1,0:T(8,128)S(1)}, f32[1,2,2,32,256]{4,3,2,1,0:T(8,128)S(1)}, u32[]{:S(2)}, u32[]{:S(2)}) collective-permute-start(f32[1,2,2,32,256]{4,3,2,1,0:T(8,128)S(1)} %dynamic-slice_bitcast_fusion.1), channel_id=1, source_target_pairs={{0,16},{4,20},{8,24},{12,28},{16,0},{20,4},{24,8},{28,12},{1,17},{... | collective-permute-start | bytes 393224 | tf_op jit(solution)/shard_map/ppermute | solution.py:128
  174.2 0.7 copy.413
  174.9 0.7 reshape.136
  175.6 6.1 %collective-permute-done.16 = f32[1,2,2,32,256]{4,3,2,1,0:T(8,128)S(1)} collective-permute-done((f32[1,2,2,32,256]{4,3,2,1,0:T(8,128)S(1)}, f32[1,2,2,32,256]{4,3,2,1,0:T(8,128)S(1)}, u32[]{:S(2)}, u32[]{:S(2)}) %collective-permute-start.16) | collective-permute-done | bytes 131104 | tf_op jit(solution)/shard_map/ppermute | solution.py:128
  181.7 0.7 copy.414
  (74 shorter events, 6.3 us)
Async XLA Ops:
  1.4 3.0 %collective-permute-start = (bf16[1,4,1,4,512]{4,3,2,1,0:T(4,128)(2,1)S(1)}, bf16[1,4,1,4,512]{4,3,2,1,0:T(4,128)(2,1)S(1)}, u32[]{:S(2)}, u32[]{:S(2)}) collective-permute-start(bf16[1,4,1,4,512]{4,3,2,1,0:T(4,128)(2,1)S(1)} %get-tuple-element.60), channel_id=1, source_target_pairs={{0,32},{32,64},{64,96},{96,128},{128,160},{160,192},{192,224},{224... | collective-permute-start | bytes 49160 | tf_op jit(solution)/shard_map/ppermute | solution.py:15
  3.1 4.4 %collective-permute-start.1 = (bf16[1,4,1,4,512]{4,3,2,1,0:T(4,128)(2,1)S(1)}, bf16[1,4,1,4,512]{4,3,2,1,0:T(4,128)(2,1)S(1)}, u32[]{:S(2)}, u32[]{:S(2)}) collective-permute-start(bf16[1,4,1,4,512]{4,3,2,1,0:T(4,128)(2,1)S(1)} %get-tuple-element.59), channel_id=1, source_target_pairs={{32,0},{64,32},{96,64},{128,96},{160,128},{192,160},{224,192},{256... | collective-permute-start | bytes 49160 | tf_op jit(solution)/shard_map/ppermute | solution.py:18
  7.6 8.8 %collective-permute-start.2 = (bf16[1,4,6,1,512]{4,3,2,1,0:T(2,128)(2,1)S(1)}, bf16[1,4,6,1,512]{4,3,2,1,0:T(2,128)(2,1)S(1)}, u32[]{:S(2)}, u32[]{:S(2)}) collective-permute-start(bf16[1,4,6,1,512]{4,3,2,1,0:T(2,128)(2,1)S(1)} %get-tuple-element.57), channel_id=1, source_target_pairs={{0,4},{4,8},{8,12},{12,16},{16,20},{20,24},{24,28},{1,5},{5,9},{9,... | collective-permute-start | bytes 73736 | tf_op jit(solution)/shard_map/ppermute | solution.py:15
  11.1 6.0 %collective-permute-start.3 = (bf16[1,4,6,1,512]{4,3,2,1,0:T(2,128)(2,1)S(1)}, bf16[1,4,6,1,512]{4,3,2,1,0:T(2,128)(2,1)S(1)}, u32[]{:S(2)}, u32[]{:S(2)}) collective-permute-start(bf16[1,4,6,1,512]{4,3,2,1,0:T(2,128)(2,1)S(1)} %get-tuple-element.58), channel_id=1, source_target_pairs={{4,0},{8,4},{12,8},{16,12},{20,16},{24,20},{28,24},{5,1},{9,5},{13... | collective-permute-start | bytes 73736 | tf_op jit(solution)/shard_map/ppermute | solution.py:18
  35.1 0.7 copy-start.1
  45.3 31.0 %copy-start.3 = (bf16[8,864]{1,0:T(8,128)(2,1)S(1)}, bf16[8,864]{1,0:T(8,128)(2,1)}, u32[]{:S(2)}) copy-start(bf16[8,864]{1,0:T(8,128)(2,1)} %param.6) | copy-start | bytes 41476
  45.3 32.8 %copy-start.2 = (bf16[1,8,1,1024]{3,1,2,0:T(8,128)(2,1)S(1)}, bf16[1,8,1,1024]{3,1,2,0:T(8,128)(2,1)}, u32[]{:S(2)}) copy-start(bf16[1,8,1,1024]{3,1,2,0:T(8,128)(2,1)} %param.7) | copy-start | bytes 49156
  73.5 5.6 %collective-permute-start.4 = (bf16[1,32,1,16,256]{4,1,3,2,0:T(8,128)(2,1)S(1)}, bf16[1,32,1,16,256]{4,1,3,2,0:T(8,128)(2,1)S(1)}, u32[]{:S(2)}, u32[]{:S(2)}) collective-permute-start(bf16[1,32,1,16,256]{4,1,3,2,0:T(8,128)(2,1)S(1)} %get-tuple-element.41), channel_id=1, source_target_pairs={{0,32},{32,64},{64,96},{96,128},{128,160},{160,192},{192,224},{224... | collective-permute-start | bytes 786440 | tf_op jit(solution)/shard_map/ppermute | solution.py:15
  74.8 6.0 %collective-permute-start.5 = (bf16[1,32,1,16,256]{4,1,3,2,0:T(8,128)(2,1)S(1)}, bf16[1,32,1,16,256]{4,1,3,2,0:T(8,128)(2,1)S(1)}, u32[]{:S(2)}, u32[]{:S(2)}) collective-permute-start(bf16[1,32,1,16,256]{4,1,3,2,0:T(8,128)(2,1)S(1)} %get-tuple-element.42), channel_id=1, source_target_pairs={{32,0},{64,32},{96,64},{128,96},{160,128},{192,160},{224,192},{256... | collective-permute-start | bytes 786440 | tf_op jit(solution)/shard_map/ppermute | solution.py:18
  83.8 2.8 %copy-start = (bf16[8,3,32,3,3]{2,0,4,3,1:T(8,128)(2,1)S(1)}, bf16[8,3,32,3,3]{2,0,4,3,1:T(8,128)(2,1)}, u32[]{:S(2)}) copy-start(bf16[8,3,32,3,3]{2,0,4,3,1:T(8,128)(2,1)} %copy.405) | copy-start | bytes 41476
  89.3 8.2 %collective-permute-start.12 = (bf16[1,8,1,16,256]{4,1,3,2,0:T(8,128)(2,1)S(1)}, bf16[1,8,1,16,256]{4,1,3,2,0:T(8,128)(2,1)S(1)}, u32[]{:S(2)}, u32[]{:S(2)}) collective-permute-start(bf16[1,8,1,16,256]{4,1,3,2,0:T(8,128)(2,1)S(1)} %get-tuple-element.55), channel_id=1, source_target_pairs={{0,32},{32,64},{64,96},{96,128},{128,160},{160,192},{192,224},{224... | collective-permute-start | bytes 196616 | tf_op jit(solution)/shard_map/ppermute | solution.py:15
  96.0 3.1 %collective-permute-start.13 = (bf16[1,8,1,16,256]{4,1,3,2,0:T(8,128)(2,1)S(1)}, bf16[1,8,1,16,256]{4,1,3,2,0:T(8,128)(2,1)S(1)}, u32[]{:S(2)}, u32[]{:S(2)}) collective-permute-start(bf16[1,8,1,16,256]{4,1,3,2,0:T(8,128)(2,1)S(1)} %get-tuple-element.56), channel_id=1, source_target_pairs={{32,0},{64,32},{96,64},{128,96},{160,128},{192,160},{224,192},{256... | collective-permute-start | bytes 196616 | tf_op jit(solution)/shard_map/ppermute | solution.py:18
  101.6 15.0 %collective-permute-start.14 = (f32[2,2,1,2,2,32,256]{6,5,4,3,0,2,1:T(8,128)S(1)}, f32[2,2,1,2,2,32,256]{6,5,4,3,0,2,1:T(8,128)S(1)}, u32[]{:S(2)}, u32[]{:S(2)}) collective-permute-start(f32[2,2,1,2,2,32,256]{6,5,4,3,0,2,1:T(8,128)S(1)} %copy.444), channel_id=1, source_target_pairs={{0,4},{4,0},{8,12},{12,8},{16,20},{20,16},{24,28},{28,24},{1,5},{5... | collective-permute-start | bytes 1572872 | tf_op jit(solution)/shard_map/ppermute | solution.py:128
  116.7 51.9 %collective-permute-start.15 = (f32[2,1,2,2,32,256]{5,4,3,2,0,1:T(8,128)S(1)}, f32[2,1,2,2,32,256]{5,4,3,2,0,1:T(8,128)}, u32[]{:S(2)}, u32[]{:S(2)}) collective-permute-start(f32[2,1,2,2,32,256]{5,4,3,2,0,1:T(8,128)S(1)} %dynamic-slice_bitcast_fusion), channel_id=1, source_target_pairs={{0,8},{4,12},{8,0},{12,4},{16,24},{20,28},{24,16},{28,20},{1,9},{5... | collective-permute-start | bytes 786440 | tf_op jit(solution)/shard_map/ppermute | solution.py:128
  124.7 7.9 %collective-permute-start.6 = (f32[54,128]{1,0:T(8,128)S(1)}, f32[54,128]{1,0:T(8,128)S(1)}, u32[]{:S(2)}, u32[]{:S(2)}) collective-permute-start(f32[54,128]{1,0:T(8,128)S(1)} %mul.80), channel_id=1, source_target_pairs={{0,1},{1,0},{2,3},{3,2},{32,33},{33,32},{34,35},{35,34},{64,65},{6... | collective-permute-start | bytes 82952 | tf_op jit(solution)/shard_map/ppermute | solution.py:42
  132.6 11.5 %collective-permute-start.7 = (f32[54,128]{1,0:T(8,128)S(1)}, f32[54,128]{1,0:T(8,128)S(1)}, u32[]{:S(2)}, u32[]{:S(2)}) collective-permute-start(f32[54,128]{1,0:T(8,128)S(1)} %add.86), channel_id=1, source_target_pairs={{0,3},{1,2},{2,1},{3,0},{32,35},{33,34},{34,33},{35,32},{64,67},{6... | collective-permute-start | bytes 82952 | tf_op jit(solution)/shard_map/ppermute | solution.py:42
  144.1 3.1 %collective-permute-start.8 = (f32[54,128]{1,0:T(8,128)S(1)}, f32[54,128]{1,0:T(8,128)S(1)}, u32[]{:S(2)}, u32[]{:S(2)}) collective-permute-start(f32[54,128]{1,0:T(8,128)S(1)} %add.87), channel_id=1, source_target_pairs={{0,32},{1,33},{2,34},{3,35},{32,0},{33,1},{34,2},{35,3},{64,96},{6... | collective-permute-start | bytes 82952 | tf_op jit(solution)/shard_map/ppermute | solution.py:42
  147.2 7.2 %collective-permute-start.9 = (f32[54,128]{1,0:T(8,128)S(1)}, f32[54,128]{1,0:T(8,128)S(1)}, u32[]{:S(2)}, u32[]{:S(2)}) collective-permute-start(f32[54,128]{1,0:T(8,128)S(1)} %add.88), channel_id=1, source_target_pairs={{0,64},{1,65},{2,66},{3,67},{32,96},{33,97},{34,98},{35,99},{64,0}... | collective-permute-start | bytes 82952 | tf_op jit(solution)/shard_map/ppermute | solution.py:42
  155.0 9.3 %collective-permute-start.10 = (f32[54,128]{1,0:T(8,128)}, f32[54,128]{1,0:T(8,128)}, u32[]{:S(2)}, u32[]{:S(2)}) collective-permute-start(f32[54,128]{1,0:T(8,128)} %add.89), channel_id=1, source_target_pairs={{0,192},{1,193},{2,194},{3,195},{32,224},{33,225},{34,226},{35,227... | collective-permute-start | bytes 82952 | tf_op jit(solution)/shard_map/ppermute | solution.py:42
  165.1 9.8 %collective-permute-start.11 = (f32[54,128]{1,0:T(8,128)S(1)}, f32[54,128]{1,0:T(8,128)S(1)}, u32[]{:S(2)}, u32[]{:S(2)}) collective-permute-start(f32[54,128]{1,0:T(8,128)S(1)} %add.90), channel_id=1, source_target_pairs={{0,256},{1,257},{2,258},{3,259},{32,288},{33,289},{34,290},{35,291... | collective-permute-start | bytes 82952 | tf_op jit(solution)/shard_map/ppermute | solution.py:42
  169.5 12.1 %collective-permute-start.16 = (f32[1,2,2,32,256]{4,3,2,1,0:T(8,128)S(1)}, f32[1,2,2,32,256]{4,3,2,1,0:T(8,128)S(1)}, u32[]{:S(2)}, u32[]{:S(2)}) collective-permute-start(f32[1,2,2,32,256]{4,3,2,1,0:T(8,128)S(1)} %dynamic-slice_bitcast_fusion.1), channel_id=1, source_target_pairs={{0,16},{4,20},{8,24},{12,28},{16,0},{20,4},{24,8},{28,12},{1,17},{... | collective-permute-start | bytes 393224 | tf_op jit(solution)/shard_map/ppermute | solution.py:128
where the time goes:
time: 184 us; the launch traced here: 182 us
  starting transfers between devices  65.5 us (36%)
  local copies, waits for them, and re-layouts  39.8 us (22%)
  waiting for transfers between devices  31.5 us (17%)
  blocking collectives  27.9 us (15%)
  other arithmetic  10.1 us (5%)
  matrix products  6.18 us (3%)
    ppermute x6, starting transfers between devices, butterfly_sum(): values = values + lax.ppermute(values, axes, pairs)  33.4 us
    all_gather x1, blocking collectives, shards(): slab_rows = lax.all_gather(level_loc, 'height', axis=3, tiled=True)  27.9 us
    ppermute x3, waiting for transfers between devices, near_first_scatter(): grid = jnp.squeeze(keep + lax.ppermute(send, axis, pairs), axis_pos)  18.7 us
    another operation x14, local copies, waits for them, and re-layouts, delta_shifts(): jnp.stack([dpad[:, :, 2 - kh:2 - kh + hsize, 2 - kw:2 - kw + wsize] for k...  18.5 us
    ppermute x4, starting transfers between devices, extended(): lax.ppermute(lax.slice_in_dim(block, block.shape[dim] - width, None, axis...  13.2 us
    ppermute x3, starting transfers between devices, near_first_scatter(): grid = jnp.squeeze(keep + lax.ppermute(send, axis, pairs), axis_pos)  11.1 us
    ppermute x4, starting transfers between devices, extended(): lax.ppermute(lax.slice_in_dim(block, 0, width, axis=dim), axis, backward)  7.84 us
    unnamed x37, local copies, waits for them, and re-layouts  7.03 us
  transfers between devices with their start and end apart: 17, of which 10 were waited for; matrix products, arithmetic and copies ran while one was open for 8% of the time, Pallas kernels for 0%

commit v1 on v0

--- a/solution.py
+++ b/solution.py
@@ -5,6 +5,9 @@
 
 LEAK_SLOPE = 0.3
 CONV_DIMS = ("NCDHW", "OIDHW", "NCDHW")
+numbers_produce = lambda mine_x: jnp.concatenate(
+    lax.all_to_all(jnp.stack([mine_x] * lax.axis_size("height"), 0), "height", 0, 0), 3
+)
 
 
 def extended(block, sides, width):
@@ -186,7 +189,7 @@
     padded = extended(volume, (("depth", 2), ("height", 3)), 1)
     pre_one = forward_product(padded, first_kernel)[:, :, :, 1:-1]
     level_loc = pooled(activate(pre_one)).astype(jnp.bfloat16)
-    slab_rows = lax.all_gather(level_loc, "height", axis=3, tiled=True)
+    slab_rows = numbers_produce(level_loc)
     level_one = extended(slab_rows, (("depth", 2),), 1)
     pre_two = forward_product(level_one, second_kernel)
     pooled_grid = pooled(activate(pre_two)).astype(jnp.bfloat16)

time: 184 us -> 178 us (0.967)
  the two profiles are of different devices: /device:TPU:8 before, /device:TPU:16 now
where the time goes in v1:
time: 178 us; the launch traced here: 176 us
  starting transfers between devices  63.7 us (36%)
  local copies, waits for them, and re-layouts  39.9 us (22%)
  waiting for transfers between devices  32.6 us (18%)
  blocking collectives  22.5 us (13%)
  other arithmetic  10.1 us (6%)
  matrix products  6.18 us (3%)
    ppermute x6, starting transfers between devices, butterfly_sum(): values = values + lax.ppermute(values, axes, pairs)  33.4 us
    all_to_all x1, blocking collectives, lax.all_to_all(jnp.stack([mine_x] * lax.axis_size('height'), 0), 'height'...  22.5 us
    ppermute x3, waiting for transfers between devices, near_first_scatter(): grid = jnp.squeeze(keep + lax.ppermute(send, axis, pairs), axis_pos)  18.8 us
    another operation x14, local copies, waits for them, and re-layouts, delta_shifts(): jnp.stack([dpad[:, :, 2 - kh:2 - kh + hsize, 2 - kw:2 - kw + wsize] for k...  18.5 us
    ppermute x4, starting transfers between devices, extended(): lax.ppermute(lax.slice_in_dim(block, block.shape[dim] - width, None, axis...  13.6 us
    ppermute x3, starting transfers between devices, near_first_scatter(): grid = jnp.squeeze(keep + lax.ppermute(send, axis, pairs), axis_pos)  10.3 us
    ppermute x4, waiting for transfers between devices, extended(): lax.ppermute(lax.slice_in_dim(block, 0, width, axis=dim), axis, backward)  7.08 us
    unnamed x37, local copies, waits for them, and re-layouts  7.03 us
  transfers between devices with their start and end apart: 17, of which 10 were waited for; matrix products, arithmetic and copies ran while one was open for 9% of the time, Pallas kernels for 0%

profile of v1, /device:TPU:16, one launch (start us, length us, event | category | flops | bytes accessed | tf_op | source)
XLA Modules:
  0.0 176.3 jit_solution(18061890987847699139)
XLA Ops:
  0.6 0.8 fusion.119
  1.4 1.7 collective-permute-start
  3.1 1.3 collective-permute-start.1
  4.5 0.9 constant_dynamic-update-slice_fusion.1
  5.3 2.2 %collective-permute-done.1 = bf16[1,4,1,4,512]{4,3,2,1,0:T(4,128)(2,1)S(1)} collective-permute-done((bf16[1,4,1,4,512]{4,3,2,1,0:T(4,128)(2,1)S(1)}, bf16[1,4,1,4,512]{4,3,2,1,0:T(4,128)(2,1)S(1)}, u32[]{:S(2)}, u32[]{:S(2)}) %collective-permute-start.1) | collective-permute-done | bytes 16416 | tf_op jit(solution)/shard_map/ppermute | solution.py:21
  7.6 3.5 %collective-permute-start.2 = (bf16[1,4,6,1,512]{4,3,2,1,0:T(2,128)(2,1)S(1)}, bf16[1,4,6,1,512]{4,3,2,1,0:T(2,128)(2,1)S(1)}, u32[]{:S(2)}, u32[]{:S(2)}) collective-permute-start(bf16[1,4,6,1,512]{4,3,2,1,0:T(2,128)(2,1)S(1)} %get-tuple-element.60), channel_id=1, source_target_pairs={{0,4},{4,8},{8,12},{12,16},{16,20},{20,24},{24,28},{1,5},{5,9},{9,... | collective-permute-start | bytes 73736 | tf_op jit(solution)/shard_map/ppermute | solution.py:18
  11.1 2.4 %collective-permute-start.3 = (bf16[1,4,6,1,512]{4,3,2,1,0:T(2,128)(2,1)S(1)}, bf16[1,4,6,1,512]{4,3,2,1,0:T(2,128)(2,1)S(1)}, u32[]{:S(2)}, u32[]{:S(2)}) collective-permute-start(bf16[1,4,6,1,512]{4,3,2,1,0:T(2,128)(2,1)S(1)} %get-tuple-element.61), channel_id=1, source_target_pairs={{4,0},{8,4},{12,8},{16,12},{20,16},{24,20},{28,24},{5,1},{9,5},{13... | collective-permute-start | bytes 73736 | tf_op jit(solution)/shard_map/ppermute | solution.py:21
  13.4 0.8 copy.436
  14.4 0.6 copy.437
  15.0 2.8 %collective-permute-done.3 = bf16[1,4,6,1,512]{4,3,2,1,0:T(2,128)(2,1)S(1)} collective-permute-done((bf16[1,4,6,1,512]{4,3,2,1,0:T(2,128)(2,1)S(1)}, bf16[1,4,6,1,512]{4,3,2,1,0:T(2,128)(2,1)S(1)}, u32[]{:S(2)}, u32[]{:S(2)}) %collective-permute-start.3) | collective-permute-done | bytes 24608 | tf_op jit(solution)/shard_map/ppermute | solution.py:21
  18.0 0.7 fusion.89
  19.7 0.9 copy.430
  20.6 0.9 copy.431
  21.6 1.0 copy.432
  22.6 0.9 copy.433
  23.5 0.9 copy.429
  24.4 11.4 %stack.179 = bf16[4,9,6,6,512]{4,1,0,3,2:T(8,128)(2,1)S(1)} concatenate(bf16[4,1,6,6,512]{4,1,0,3,2:T(2,128)(2,1)S(1)} %copy.425, bf16[4,1,6,6,512]{4,1,0,3,2:T(2,128)(2,1)S(1)} %copy.426, bf16[4,1,6,6,512]{4,1,0,3,2:T(2,128)(2,1)S(1)} %copy.427, bf16[4,1,6,6,512]{4,1,0,3,2:T(2,128)(2,1)S(1)} %copy.428, bf16[4,1,6,6,512]{4,1,0,3,2:T(2,128)(2,1)} %copy.429, ...), dimensions={1} | concatenate | bytes 2654208 | tf_op jit(solution)/shard_map/stack | solution.py:70
  35.9 0.6 slice_bitcast_fusion.5
  36.6 1.4 fusion.27
  38.0 0.6 fusion.61
  38.7 2.6 %copy.439 = f32[1,32,4,4,512]{1,4,3,2,0:T(8,128)} copy(f32[1,32,4,4,512]{4,1,3,2,0:T(8,128)S(1)} %fusion.61) | data formatting | bytes 2097152 | tf_op jit(solution)/shard_map/add | solution.py:136
  41.3 4.8 %reduce_sum.21 = f32[32,2,2,256]{0,3,2,1:T(8,128)S(1)} reduce(f32[32,2,2,2,2,256,2]{0,6,5,4,3,2,1:T(2,128)} %bitcast.267, f32[]{:T(128)} %constant.17.clone.1), dimensions={2,4,6}, to_apply=%region_0.1 | reduce | flops 229376 | bytes 1179652 | tf_op jit(solution)/shard_map/reduce_sum | solution.py:146
  46.4 22.5 %all_to_all.5 = bf16[8,1,32,2,2,256]{5,2,4,3,1,0:T(8,128)(2,1)S(1)} all-to-all(bf16[8,1,32,2,2,256]{5,2,4,3,1,0:T(8,128)(2,1)S(1)} %stack.184), channel_id=1, replica_groups=mesh['depth'=16,'height'=8,'sample'=4] {'height'}, dimensions={0} | all-to-all | bytes 1048576 | tf_op jit(solution)/shard_map/all_to_all | solution.py:9
  68.9 1.7 collective-permute-start.4
  70.6 1.5 collective-permute-start.5
  72.5 0.7 rev.9
  73.2 0.8 copy.453
  74.9 0.5 collective-permute-done.5
  76.0 0.4 fusion.49
  76.4 0.4 fusion.51
  77.0 0.5 fusion.53
  77.9 0.4 fusion.59
  78.4 2.8 %slice_bitcast_fusion.2 = (bf16[1,32,9,2,16,256]{5,1,2,0,4,3:T(8,128)(2,1)S(1)}, bf16[1,32,9,2,16,256]{5,1,2,0,4,3:T(8,128)(2,1)S(1)}, bf16[1,32,9,2,16,256]{5,1,2,0,4,3:T(8,128)(2,1)S(1)}) fusion(bf16[32,9,4,16,256]{4,0,1,3,2:T(8,128)(2,1)S(1)} %fusion.59), kind=kLoop, calls=%fused_computation.8 | loop fusion | bytes 28311552 | tf_op jit(solution)/shard_map/stack | solution.py:106
  81.2 2.6 %multiply_convert_fusion.1 = (bf16[8,2,16,256]{3,0,2,1:T(8,128)(2,1)S(1)}, f32[8,16,256]{2,0,1:T(8,128)S(1)}) fusion(f32[8,16,256]{2,0,1:T(8,128)S(1)} %copy.456, bf16[8,3,32,9,1,1]{2,0,3,1,5,4:T(8,128)(2,1)S(1)} %bitcast.283, bf16[1,32,9,2,16,256]{5,1,2,0,4,3:T(8,128)(2,1)S(1)} %get-tuple-element.34, ...), kind=kOutput, calls=%fused_computation.113 | convolution fusion | flops 128483328 | bytes 14562816 | tf_op jit(solution)/shard_map/dot_general | solution.py:109
  83.9 6.7 %collective-permute-start.12 = (bf16[1,8,1,16,256]{4,1,3,2,0:T(8,128)(2,1)S(1)}, bf16[1,8,1,16,256]{4,1,3,2,0:T(8,128)(2,1)S(1)}, u32[]{:S(2)}, u32[]{:S(2)}) collective-permute-start(bf16[1,8,1,16,256]{4,1,3,2,0:T(8,128)(2,1)S(1)} %get-tuple-element.58), channel_id=1, source_target_pairs={{0,32},{32,64},{64,96},{96,128},{128,160},{160,192},{192,224},{224... | collective-permute-start | bytes 196616 | tf_op jit(solution)/shard_map/ppermute | solution.py:18
  90.6 1.3 collective-permute-start.13
  92.2 1.6 collective-permute-done.13
  95.1 0.9 fusion.12
  96.2 2.8 %collective-permute-start.14 = (f32[2,2,1,2,2,32,256]{6,5,4,3,0,2,1:T(8,128)S(1)}, f32[2,2,1,2,2,32,256]{6,5,4,3,0,2,1:T(8,128)S(1)}, u32[]{:S(2)}, u32[]{:S(2)}) collective-permute-start(f32[2,2,1,2,2,32,256]{6,5,4,3,0,2,1:T(8,128)S(1)} %copy.492), channel_id=1, source_target_pairs={{0,4},{4,0},{8,12},{12,8},{16,20},{20,16},{24,28},{28,24},{1,5},{5... | collective-permute-start | bytes 1572872 | tf_op jit(solution)/shard_map/ppermute | solution.py:131
  99.4 11.9 %collective-permute-done.14 = f32[2,2,1,2,2,32,256]{6,5,4,3,0,2,1:T(8,128)S(1)} collective-permute-done((f32[2,2,1,2,2,32,256]{6,5,4,3,0,2,1:T(8,128)S(1)}, f32[2,2,1,2,2,32,256]{6,5,4,3,0,2,1:T(8,128)S(1)}, u32[]{:S(2)}, u32[]{:S(2)}) %collective-permute-start.14) | collective-permute-done | bytes 524320 | tf_op jit(solution)/shard_map/ppermute | solution.py:131
  111.4 5.0 %collective-permute-start.15 = (f32[2,1,2,2,32,256]{5,4,3,2,0,1:T(8,128)S(1)}, f32[2,1,2,2,32,256]{5,4,3,2,0,1:T(8,128)}, u32[]{:S(2)}, u32[]{:S(2)}) collective-permute-start(f32[2,1,2,2,32,256]{5,4,3,2,0,1:T(8,128)S(1)} %dynamic-slice_bitcast_fusion), channel_id=1, source_target_pairs={{0,8},{4,12},{8,0},{12,4},{16,24},{20,28},{24,16},{28,20},{1,9},{5... | collective-permute-start | bytes 786440 | tf_op jit(solution)/shard_map/ppermute | solution.py:131
  116.4 1.2 fusion.39
  117.6 1.2 copy.457
  118.8 1.0 mul.80
  119.8 6.1 %collective-permute-start.6 = (f32[54,128]{1,0:T(8,128)S(1)}, f32[54,128]{1,0:T(8,128)S(1)}, u32[]{:S(2)}, u32[]{:S(2)}) collective-permute-start(f32[54,128]{1,0:T(8,128)S(1)} %mul.80), channel_id=1, source_target_pairs={{0,1},{1,0},{2,3},{3,2},{32,33},{33,32},{34,35},{35,34},{64,65},{6... | collective-permute-start | bytes 82952 | tf_op jit(solution)/shard_map/ppermute | solution.py:45
  125.9 1.8 %collective-permute-done.6 = f32[54,128]{1,0:T(8,128)S(1)} collective-permute-done((f32[54,128]{1,0:T(8,128)S(1)}, f32[54,128]{1,0:T(8,128)S(1)}, u32[]{:S(2)}, u32[]{:S(2)}) %collective-permute-start.6) | collective-permute-done | bytes 27680 | tf_op jit(solution)/shard_map/ppermute | solution.py:45
  127.7 9.8 %collective-permute-start.7 = (f32[54,128]{1,0:T(8,128)S(1)}, f32[54,128]{1,0:T(8,128)S(1)}, u32[]{:S(2)}, u32[]{:S(2)}) collective-permute-start(f32[54,128]{1,0:T(8,128)S(1)} %add.86), channel_id=1, source_target_pairs={{0,3},{1,2},{2,1},{3,0},{32,35},{33,34},{34,33},{35,32},{64,67},{6... | collective-permute-start | bytes 82952 | tf_op jit(solution)/shard_map/ppermute | solution.py:45
  137.5 1.8 %collective-permute-done.7 = f32[54,128]{1,0:T(8,128)S(1)} collective-permute-done((f32[54,128]{1,0:T(8,128)S(1)}, f32[54,128]{1,0:T(8,128)S(1)}, u32[]{:S(2)}, u32[]{:S(2)}) %collective-permute-start.7) | collective-permute-done | bytes 27680 | tf_op jit(solution)/shard_map/ppermute | solution.py:45
  139.4 1.9 %collective-permute-start.8 = (f32[54,128]{1,0:T(8,128)S(1)}, f32[54,128]{1,0:T(8,128)S(1)}, u32[]{:S(2)}, u32[]{:S(2)}) collective-permute-start(f32[54,128]{1,0:T(8,128)S(1)} %add.87), channel_id=1, source_target_pairs={{0,32},{1,33},{2,34},{3,35},{32,0},{33,1},{34,2},{35,3},{64,96},{6... | collective-permute-start | bytes 82952 | tf_op jit(solution)/shard_map/ppermute | solution.py:45
  141.3 1.2 collective-permute-done.8
  142.5 5.0 %collective-permute-start.9 = (f32[54,128]{1,0:T(8,128)S(1)}, f32[54,128]{1,0:T(8,128)S(1)}, u32[]{:S(2)}, u32[]{:S(2)}) collective-permute-start(f32[54,128]{1,0:T(8,128)S(1)} %add.88), channel_id=1, source_target_pairs={{0,64},{1,65},{2,66},{3,67},{32,96},{33,97},{34,98},{35,99},{64,0}... | collective-permute-start | bytes 82952 | tf_op jit(solution)/shard_map/ppermute | solution.py:45
  147.5 1.8 %collective-permute-done.9 = f32[54,128]{1,0:T(8,128)S(1)} collective-permute-done((f32[54,128]{1,0:T(8,128)S(1)}, f32[54,128]{1,0:T(8,128)S(1)}, u32[]{:S(2)}, u32[]{:S(2)}) %collective-permute-start.9) | collective-permute-done | bytes 27680 | tf_op jit(solution)/shard_map/ppermute | solution.py:45
  149.3 0.6 add.89
  149.9 4.9 %collective-permute-start.10 = (f32[54,128]{1,0:T(8,128)}, f32[54,128]{1,0:T(8,128)}, u32[]{:S(2)}, u32[]{:S(2)}) collective-permute-start(f32[54,128]{1,0:T(8,128)} %add.89), channel_id=1, source_target_pairs={{0,192},{1,193},{2,194},{3,195},{32,224},{33,225},{34,226},{35,227... | collective-permute-start | bytes 82952 | tf_op jit(solution)/shard_map/ppermute | solution.py:45
  154.9 0.6 copy.454
  155.5 1.7 reduce_sum.28
  157.2 0.8 add.90
  158.0 5.7 %collective-permute-start.11 = (f32[54,128]{1,0:T(8,128)S(1)}, f32[54,128]{1,0:T(8,128)S(1)}, u32[]{:S(2)}, u32[]{:S(2)}) collective-permute-start(f32[54,128]{1,0:T(8,128)S(1)} %add.90), channel_id=1, source_target_pairs={{0,256},{1,257},{2,258},{3,259},{32,288},{33,289},{34,290},{35,291... | collective-permute-start | bytes 82952 | tf_op jit(solution)/shard_map/ppermute | solution.py:45
  163.6 1.0 bitcast_add_fusion
  164.7 2.5 %collective-permute-start.16 = (f32[1,2,2,32,256]{4,3,2,1,0:T(8,128)S(1)}, f32[1,2,2,32,256]{4,3,2,1,0:T(8,128)S(1)}, u32[]{:S(2)}, u32[]{:S(2)}) collective-permute-start(f32[1,2,2,32,256]{4,3,2,1,0:T(8,128)S(1)} %dynamic-slice_bitcast_fusion.1), channel_id=1, source_target_pairs={{0,16},{4,20},{8,24},{12,28},{16,0},{20,4},{24,8},{28,12},{1,17},{... | collective-permute-start | bytes 393224 | tf_op jit(solution)/shard_map/ppermute | solution.py:131
  167.2 0.7 copy.461
  167.9 0.7 reshape.138
  168.6 6.9 %collective-permute-done.16 = f32[1,2,2,32,256]{4,3,2,1,0:T(8,128)S(1)} collective-permute-done((f32[1,2,2,32,256]{4,3,2,1,0:T(8,128)S(1)}, f32[1,2,2,32,256]{4,3,2,1,0:T(8,128)S(1)}, u32[]{:S(2)}, u32[]{:S(2)}) %collective-permute-start.16) | collective-permute-done | bytes 131104 | tf_op jit(solution)/shard_map/ppermute | solution.py:131
  175.6 0.7 copy.462
  (76 shorter events, 6.4 us)
Async XLA Ops:
  1.4 3.0 %collective-permute-start = (bf16[1,4,1,4,512]{4,3,2,1,0:T(4,128)(2,1)S(1)}, bf16[1,4,1,4,512]{4,3,2,1,0:T(4,128)(2,1)S(1)}, u32[]{:S(2)}, u32[]{:S(2)}) collective-permute-start(bf16[1,4,1,4,512]{4,3,2,1,0:T(4,128)(2,1)S(1)} %get-tuple-element.63), channel_id=1, source_target_pairs={{0,32},{32,64},{64,96},{96,128},{128,160},{160,192},{192,224},{224... | collective-permute-start | bytes 49160 | tf_op jit(solution)/shard_map/ppermute | solution.py:18
  3.1 4.4 %collective-permute-start.1 = (bf16[1,4,1,4,512]{4,3,2,1,0:T(4,128)(2,1)S(1)}, bf16[1,4,1,4,512]{4,3,2,1,0:T(4,128)(2,1)S(1)}, u32[]{:S(2)}, u32[]{:S(2)}) collective-permute-start(bf16[1,4,1,4,512]{4,3,2,1,0:T(4,128)(2,1)S(1)} %get-tuple-element.62), channel_id=1, source_target_pairs={{32,0},{64,32},{96,64},{128,96},{160,128},{192,160},{224,192},{256... | collective-permute-start | bytes 49160 | tf_op jit(solution)/shard_map/ppermute | solution.py:21
  7.6 7.4 %collective-permute-start.2 = (bf16[1,4,6,1,512]{4,3,2,1,0:T(2,128)(2,1)S(1)}, bf16[1,4,6,1,512]{4,3,2,1,0:T(2,128)(2,1)S(1)}, u32[]{:S(2)}, u32[]{:S(2)}) collective-permute-start(bf16[1,4,6,1,512]{4,3,2,1,0:T(2,128)(2,1)S(1)} %get-tuple-element.60), channel_id=1, source_target_pairs={{0,4},{4,8},{8,12},{12,16},{16,20},{20,24},{24,28},{1,5},{5,9},{9,... | collective-permute-start | bytes 73736 | tf_op jit(solution)/shard_map/ppermute | solution.py:18
  11.1 6.8 %collective-permute-start.3 = (bf16[1,4,6,1,512]{4,3,2,1,0:T(2,128)(2,1)S(1)}, bf16[1,4,6,1,512]{4,3,2,1,0:T(2,128)(2,1)S(1)}, u32[]{:S(2)}, u32[]{:S(2)}) collective-permute-start(bf16[1,4,6,1,512]{4,3,2,1,0:T(2,128)(2,1)S(1)} %get-tuple-element.61), channel_id=1, source_target_pairs={{4,0},{8,4},{12,8},{16,12},{20,16},{24,20},{28,24},{5,1},{9,5},{13... | collective-permute-start | bytes 73736 | tf_op jit(solution)/shard_map/ppermute | solution.py:21
  35.9 0.7 copy-start.1
  46.1 26.1 %copy-start.3 = (bf16[8,864]{1,0:T(8,128)(2,1)S(1)}, bf16[8,864]{1,0:T(8,128)(2,1)}, u32[]{:S(2)}) copy-start(bf16[8,864]{1,0:T(8,128)(2,1)} %param.6) | copy-start | bytes 41476
  46.3 27.6 %copy-start.2 = (bf16[1,8,1,1024]{3,1,2,0:T(8,128)(2,1)S(1)}, bf16[1,8,1,1024]{3,1,2,0:T(8,128)(2,1)}, u32[]{:S(2)}) copy-start(bf16[1,8,1,1024]{3,1,2,0:T(8,128)(2,1)} %param.7) | copy-start | bytes 49156
  68.9 6.0 %collective-permute-start.4 = (bf16[1,32,1,16,256]{4,1,3,2,0:T(8,128)(2,1)S(1)}, bf16[1,32,1,16,256]{4,1,3,2,0:T(8,128)(2,1)S(1)}, u32[]{:S(2)}, u32[]{:S(2)}) collective-permute-start(bf16[1,32,1,16,256]{4,1,3,2,0:T(8,128)(2,1)S(1)} %get-tuple-element.44), channel_id=1, source_target_pairs={{0,32},{32,64},{64,96},{96,128},{128,160},{160,192},{192,224},{224... | collective-permute-start | bytes 786440 | tf_op jit(solution)/shard_map/ppermute | solution.py:18
  70.6 4.8 %collective-permute-start.5 = (bf16[1,32,1,16,256]{4,1,3,2,0:T(8,128)(2,1)S(1)}, bf16[1,32,1,16,256]{4,1,3,2,0:T(8,128)(2,1)S(1)}, u32[]{:S(2)}, u32[]{:S(2)}) collective-permute-start(bf16[1,32,1,16,256]{4,1,3,2,0:T(8,128)(2,1)S(1)} %get-tuple-element.45), channel_id=1, source_target_pairs={{32,0},{64,32},{96,64},{128,96},{160,128},{192,160},{224,192},{256... | collective-permute-start | bytes 786440 | tf_op jit(solution)/shard_map/ppermute | solution.py:21
  78.4 2.8 %copy-start = (bf16[8,3,32,3,3]{2,0,4,3,1:T(8,128)(2,1)S(1)}, bf16[8,3,32,3,3]{2,0,4,3,1:T(8,128)(2,1)}, u32[]{:S(2)}) copy-start(bf16[8,3,32,3,3]{2,0,4,3,1:T(8,128)(2,1)} %copy.453) | copy-start | bytes 41476
  83.9 8.2 %collective-permute-start.12 = (bf16[1,8,1,16,256]{4,1,3,2,0:T(8,128)(2,1)S(1)}, bf16[1,8,1,16,256]{4,1,3,2,0:T(8,128)(2,1)S(1)}, u32[]{:S(2)}, u32[]{:S(2)}) collective-permute-start(bf16[1,8,1,16,256]{4,1,3,2,0:T(8,128)(2,1)S(1)} %get-tuple-element.58), channel_id=1, source_target_pairs={{0,32},{32,64},{64,96},{96,128},{128,160},{160,192},{192,224},{224... | collective-permute-start | bytes 196616 | tf_op jit(solution)/shard_map/ppermute | solution.py:18
  90.6 3.1 %collective-permute-start.13 = (bf16[1,8,1,16,256]{4,1,3,2,0:T(8,128)(2,1)S(1)}, bf16[1,8,1,16,256]{4,1,3,2,0:T(8,128)(2,1)S(1)}, u32[]{:S(2)}, u32[]{:S(2)}) collective-permute-start(bf16[1,8,1,16,256]{4,1,3,2,0:T(8,128)(2,1)S(1)} %get-tuple-element.59), channel_id=1, source_target_pairs={{32,0},{64,32},{96,64},{128,96},{160,128},{192,160},{224,192},{256... | collective-permute-start | bytes 196616 | tf_op jit(solution)/shard_map/ppermute | solution.py:21
  96.2 15.1 %collective-permute-start.14 = (f32[2,2,1,2,2,32,256]{6,5,4,3,0,2,1:T(8,128)S(1)}, f32[2,2,1,2,2,32,256]{6,5,4,3,0,2,1:T(8,128)S(1)}, u32[]{:S(2)}, u32[]{:S(2)}) collective-permute-start(f32[2,2,1,2,2,32,256]{6,5,4,3,0,2,1:T(8,128)S(1)} %copy.492), channel_id=1, source_target_pairs={{0,4},{4,0},{8,12},{12,8},{16,20},{20,16},{24,28},{28,24},{1,5},{5... | collective-permute-start | bytes 1572872 | tf_op jit(solution)/shard_map/ppermute | solution.py:131
  111.4 52.2 %collective-permute-start.15 = (f32[2,1,2,2,32,256]{5,4,3,2,0,1:T(8,128)S(1)}, f32[2,1,2,2,32,256]{5,4,3,2,0,1:T(8,128)}, u32[]{:S(2)}, u32[]{:S(2)}) collective-permute-start(f32[2,1,2,2,32,256]{5,4,3,2,0,1:T(8,128)S(1)} %dynamic-slice_bitcast_fusion), channel_id=1, source_target_pairs={{0,8},{4,12},{8,0},{12,4},{16,24},{20,28},{24,16},{28,20},{1,9},{5... | collective-permute-start | bytes 786440 | tf_op jit(solution)/shard_map/ppermute | solution.py:131
  119.8 7.9 %collective-permute-start.6 = (f32[54,128]{1,0:T(8,128)S(1)}, f32[54,128]{1,0:T(8,128)S(1)}, u32[]{:S(2)}, u32[]{:S(2)}) collective-permute-start(f32[54,128]{1,0:T(8,128)S(1)} %mul.80), channel_id=1, source_target_pairs={{0,1},{1,0},{2,3},{3,2},{32,33},{33,32},{34,35},{35,34},{64,65},{6... | collective-permute-start | bytes 82952 | tf_op jit(solution)/shard_map/ppermute | solution.py:45
  127.7 11.6 %collective-permute-start.7 = (f32[54,128]{1,0:T(8,128)S(1)}, f32[54,128]{1,0:T(8,128)S(1)}, u32[]{:S(2)}, u32[]{:S(2)}) collective-permute-start(f32[54,128]{1,0:T(8,128)S(1)} %add.86), channel_id=1, source_target_pairs={{0,3},{1,2},{2,1},{3,0},{32,35},{33,34},{34,33},{35,32},{64,67},{6... | collective-permute-start | bytes 82952 | tf_op jit(solution)/shard_map/ppermute | solution.py:45
  139.4 3.1 %collective-permute-start.8 = (f32[54,128]{1,0:T(8,128)S(1)}, f32[54,128]{1,0:T(8,128)S(1)}, u32[]{:S(2)}, u32[]{:S(2)}) collective-permute-start(f32[54,128]{1,0:T(8,128)S(1)} %add.87), channel_id=1, source_target_pairs={{0,32},{1,33},{2,34},{3,35},{32,0},{33,1},{34,2},{35,3},{64,96},{6... | collective-permute-start | bytes 82952 | tf_op jit(solution)/shard_map/ppermute | solution.py:45
  142.5 6.8 %collective-permute-start.9 = (f32[54,128]{1,0:T(8,128)S(1)}, f32[54,128]{1,0:T(8,128)S(1)}, u32[]{:S(2)}, u32[]{:S(2)}) collective-permute-start(f32[54,128]{1,0:T(8,128)S(1)} %add.88), channel_id=1, source_target_pairs={{0,64},{1,65},{2,66},{3,67},{32,96},{33,97},{34,98},{35,99},{64,0}... | collective-permute-start | bytes 82952 | tf_op jit(solution)/shard_map/ppermute | solution.py:45
  149.9 7.3 %collective-permute-start.10 = (f32[54,128]{1,0:T(8,128)}, f32[54,128]{1,0:T(8,128)}, u32[]{:S(2)}, u32[]{:S(2)}) collective-permute-start(f32[54,128]{1,0:T(8,128)} %add.89), channel_id=1, source_target_pairs={{0,192},{1,193},{2,194},{3,195},{32,224},{33,225},{34,226},{35,227... | collective-permute-start | bytes 82952 | tf_op jit(solution)/shard_map/ppermute | solution.py:45
  158.0 10.0 %collective-permute-start.11 = (f32[54,128]{1,0:T(8,128)S(1)}, f32[54,128]{1,0:T(8,128)S(1)}, u32[]{:S(2)}, u32[]{:S(2)}) collective-permute-start(f32[54,128]{1,0:T(8,128)S(1)} %add.90), channel_id=1, source_target_pairs={{0,256},{1,257},{2,258},{3,259},{32,288},{33,289},{34,290},{35,291... | collective-permute-start | bytes 82952 | tf_op jit(solution)/shard_map/ppermute | solution.py:45
  164.7 10.9 %collective-permute-start.16 = (f32[1,2,2,32,256]{4,3,2,1,0:T(8,128)S(1)}, f32[1,2,2,32,256]{4,3,2,1,0:T(8,128)S(1)}, u32[]{:S(2)}, u32[]{:S(2)}) collective-permute-start(f32[1,2,2,32,256]{4,3,2,1,0:T(8,128)S(1)} %dynamic-slice_bitcast_fusion.1), channel_id=1, source_target_pairs={{0,16},{4,20},{8,24},{12,28},{16,0},{20,4},{24,8},{28,12},{1,17},{... | collective-permute-start | bytes 393224 | tf_op jit(solution)/shard_map/ppermute | solution.py:131
